TPU v7x, 256 devices: a whole 4x4x8 slice. The times are simulated.
256 devices in a mesh: seq: 32 (over x, z), row: 2 (over core), col: 4 (over y).
Axes of the slice: x: 4, y: 4, z: 8, core: 2. Of those that a mesh axis runs over, the one named last changes fastest.
Arguments:
- hidden: bfloat16 [16384, 4096], P(('seq', 'row'), 'col'), may hold values from -6 to 6
- w_x: bfloat16 [4096, 4, 1024], P('col', None, 'row'), may hold values from -0.09375 to 0.09375
- w_z: bfloat16 [4096, 4, 1024], P('col', None, 'row'), may hold values from -0.09375 to 0.09375
- w_bc: bfloat16 [4096, 4, 256], P('col'), may hold values from -0.09375 to 0.09375
- w_dt: bfloat16 [4096, 4, 16], P('col', None, 'row'), may hold values from -0.09375 to 0.09375
- conv_x_w: bfloat16 [4, 4, 1024], P(None, 'col', 'row'), may hold values from -3 to 3
- conv_bc_w: bfloat16 [4, 4, 256], P(None, 'col'), may hold values from -3 to 3
- conv_x_bias: bfloat16 [4, 1024], P('col', 'row'), may hold values from -3 to 3
- conv_bc_bias: bfloat16 [4, 256], P('col'), may hold values from -3 to 3
- dt_bias: float32 [4, 16], P('col', 'row'), may hold values from -5 to -2
- decay_rate: float32 [4, 16], P('col', 'row'), may hold values from 0.005 to 2
- d_skip: float32 [4, 16], P('col', 'row'), may hold values from 0.5 to 1.5
- norm_gain: float32 [4, 1024], P('col', 'row'), may hold values from 0.5 to 1.5
- starts: int32 [16384], P('seq'), may hold values from 0 to 1, as said below
- init_states: float32 [96, 4, 16, 64, 128], P('seq', 'col', 'row'), may hold values from -1.2 to 1.2
- conv_x_edges: bfloat16 [96, 3, 4, 1024], P('seq', None, 'col', 'row'), may hold values from -6 to 6
- conv_bc_edges: bfloat16 [96, 3, 4, 256], P('seq', None, 'col'), may hold values from -6 to 6
Outputs:
- gated_out: bfloat16 [16384, 4, 1024], P('seq', 'col', 'row')
- final_states: float32 [96, 4, 16, 64, 128], P('seq', 'col', 'row')
Inputs may be any that keep to these rules, and one draw needn't show every extreme that they name: The first token of all has starts 1. The 512 tokens of one index of seq hold at most 3 ones, and some index holds exactly 3. The last two indices of seq each hold one or more ones. Slot j of an index of seq in init_states, conv_x_edges, conv_bc_edges and final_states belongs to the j-th request that begins among its tokens; the others are not read.
All inputs are finite; a program needn't handle non-finite values.
Results may differ from a plain program's by a relative error of at most 0.0057.
Values may be sent and summed in bfloat16 or wider, within the bound.
No kernel may reach another device: no remote copies, remote signals or barrier semaphores. Data moves between devices by JAX's collectives and lax.ppermute only.
A program may use at most 128 MiB of HBM per device.

v0:
```python
import jax
import jax.numpy as jnp
from jax import lax
from jax.sharding import PartitionSpec as P

P_SIZE = 64
N = 128
PRECISE = lax.Precision.HIGHEST
EPSILON = 1e-05


def from_behind(value, axis, steps):
    count = lax.axis_size(axis)
    first, last = (max(0, -steps), min(count, count - steps))
    return lax.ppermute(value, axis, [(source, source + steps) for source in range(first, last)])


def local_terms(x_vals, b_proj, c_proj, dt_vals, flag_vals, init_vals, rate_vals):
    rows_here = x_vals.shape[0]
    slot_total = init_vals.shape[0]
    positions = jnp.arange(rows_here, dtype=jnp.int32)
    segment = jnp.cumsum(flag_vals.astype(jnp.int32))
    started = segment[rows_here - 1]
    log_decay = -dt_vals * rate_vals[None, :]
    cumulative = jnp.cumsum(log_decay, axis=0)
    preceding = cumulative - log_decay
    start_at = lax.cummax(jnp.where(flag_vals, positions, 0), axis=0)
    baseline = jnp.where((segment > 0)[:, None], preceding[start_at], 0.0)
    joined = (segment[:, None] == segment[None, :]) & (positions[:, None] >= positions[None, :])
    intersection = jnp.dot(c_proj, b_proj.T, preferred_element_type=jnp.float32)
    cumul_t = cumulative.T
    spread = jnp.where(joined[None], cumul_t[:, :, None] - cumul_t[:, None, :], 0.0)
    mixing = (
        jnp.where(joined[None], jnp.exp(spread), 0.0) * intersection[None] * dt_vals.T[:, None, :]
    )
    internal = jnp.einsum("hij,jhp->ihp", mixing, x_vals.astype(jnp.float32), precision=PRECISE)
    from_slot = jnp.einsum(
        "tn,shpn->tshp", c_proj.astype(jnp.float32), init_vals, precision=PRECISE
    )
    slot_ids = jnp.arange(1, slot_total + 1, dtype=jnp.int32)
    chosen = (segment[:, None] == slot_ids[None, :]).astype(jnp.float32)
    restarted = jnp.einsum("ts,tshp->thp", chosen, from_slot, precision=PRECISE)
    y_part = internal + jnp.exp(cumulative - baseline)[:, :, None] * restarted
    carried = jnp.where((segment == 0)[:, None], jnp.exp(cumulative), 0.0)
    indices = jnp.arange(slot_total + 1, dtype=jnp.int32)
    belongs = segment[:, None] == indices[None, :]
    last_at = jnp.max(jnp.where(belongs, positions[:, None], -1), axis=0)
    first_at = jnp.min(jnp.where(belongs, positions[:, None], rows_here), axis=0)
    cumul_end = jnp.where((last_at >= 0)[:, None], cumulative[jnp.maximum(last_at, 0)], 0.0)
    lag_spread = jnp.where(belongs.T[:, :, None], cumul_end[:, None, :] - cumulative[None], 0.0)
    weights = jnp.where(belongs.T[:, :, None], jnp.exp(lag_spread), 0.0) * dt_vals[None]
    weighted = weights[..., None] * x_vals.astype(jnp.float32)[None]
    gathered = jnp.einsum("sthp,tn->shpn", weighted, b_proj.astype(jnp.float32), precision=PRECISE)
    base_slot = preceding[jnp.minimum(first_at, rows_here - 1)]
    factor = jnp.exp(jnp.where((slot_ids <= started)[:, None], cumul_end[1:] - base_slot[1:], 0.0))
    in_use = slot_ids <= started
    seg_rest = gathered[1:] + jnp.where(
        in_use[:, None, None, None], factor[..., None, None] * init_vals, 0.0
    )
    seg_ends = jnp.concatenate([gathered[:1], seg_rest], axis=0)
    decay_all = jnp.where(started == 0, jnp.exp(cumulative[rows_here - 1]), 0.0)
    state_add = jnp.sum(jnp.where((indices == started)[:, None, None, None], seg_ends, 0.0), axis=0)
    return (y_part, carried, seg_ends, decay_all, state_add, cumul_end[0], started)


def tail_rows(raw, edges, start_last, segment_last, lagged):
    rows_here = raw.shape[0]
    source = jnp.arange(rows_here - lagged, rows_here, dtype=jnp.int32)
    inside = source >= start_last
    row_pick = jnp.clip(lagged - start_last + source, 0, lagged - 1)
    from_edge = edges[jnp.maximum(segment_last - 1, 0), row_pick]
    return jnp.where(inside[:, None], raw[rows_here - lagged :], from_edge)


def convolve(raw, prior, edges, kernel, offset_bias, start_at, segment, positions, lagged):
    rows_here = raw.shape[0]
    slot_total = edges.shape[0]
    extended = jnp.concatenate([prior, raw], axis=0)
    table = edges.reshape(slot_total * lagged, edges.shape[-1])
    total = offset_bias[None].astype(jnp.float32) + kernel[lagged][None].astype(
        jnp.float32
    ) * raw.astype(jnp.float32)
    for offset in range(1, lagged + 1):
        source = positions - offset
        inside = source >= start_at
        row_pick = jnp.clip(lagged - start_at + source, 0, lagged - 1)
        which = jnp.maximum(segment - 1, 0) * lagged + row_pick
        picker = (
            which[:, None] == jnp.arange(slot_total * lagged, dtype=jnp.int32)[None, :]
        ).astype(jnp.bfloat16)
        from_edge = jnp.dot(picker, table, preferred_element_type=jnp.float32)
        earlier = extended[lagged - offset : lagged - offset + rows_here].astype(jnp.float32)
        total = total + kernel[lagged - offset][None].astype(jnp.float32) * jnp.where(
            inside[:, None], earlier, from_edge
        )
    return jax.nn.silu(total).astype(jnp.bfloat16)


def shards(
    hidden,
    w_x,
    w_z,
    w_bc,
    w_dt,
    conv_x_w,
    conv_bc_w,
    conv_x_bias,
    conv_bc_bias,
    dt_bias,
    decay_rate,
    d_skip,
    norm_gain,
    starts,
    init_states,
    conv_x_edges,
    conv_bc_edges,
):
    tokens = lax.all_gather(hidden, "row", axis=0, tiled=True)
    rows_here = tokens.shape[0]
    channels = w_x.shape[2]
    heads_here = w_dt.shape[2]
    lagged = conv_x_w.shape[0] - 1
    pieces = [
        jnp.einsum("td,dgc->gtc", tokens, weight, preferred_element_type=jnp.float32)
        for weight in (w_x, w_z, w_bc, w_dt)
    ]
    summed = lax.psum_scatter(
        jnp.concatenate(pieces, axis=2), "col", scatter_dimension=0, tiled=True
    )
    mixed = summed[0].astype(jnp.bfloat16)
    x_raw = mixed[:, :channels]
    z_gate = mixed[:, channels : 2 * channels]
    bc_raw = mixed[:, 2 * channels : 2 * channels + 2 * N]
    dt_raw = mixed[:, 2 * channels + 2 * N :]
    positions = jnp.arange(rows_here, dtype=jnp.int32)
    flag_vals = starts == 1
    segment = jnp.cumsum(starts)
    start_at = lax.cummax(jnp.where(flag_vals, positions, -lagged), axis=0)
    x_edges = conv_x_edges[:, :, 0]
    bc_edges = conv_bc_edges[:, :, 0]
    start_last = start_at[rows_here - 1]
    segment_last = segment[rows_here - 1]
    send_x = tail_rows(x_raw, x_edges, start_last, segment_last, lagged)
    send_bc = tail_rows(bc_raw, bc_edges, start_last, segment_last, lagged)
    prior_x, prior_bc = from_behind((send_x, send_bc), "seq", 1)
    x_conv = convolve(
        x_raw,
        prior_x,
        x_edges,
        conv_x_w[:, 0],
        conv_x_bias[0],
        start_at,
        segment,
        positions,
        lagged,
    )
    bc_conv = convolve(
        bc_raw,
        prior_bc,
        bc_edges,
        conv_bc_w[:, 0],
        conv_bc_bias[0],
        start_at,
        segment,
        positions,
        lagged,
    )
    x_heads = x_conv.reshape(rows_here, heads_here, P_SIZE)
    b_proj = bc_conv[:, :N]
    c_proj = bc_conv[:, N:]
    dt_vals = jax.nn.softplus(dt_raw.astype(jnp.float32) + dt_bias[0][None, :])
    init_vals = init_states[:, 0]
    y_part, carried, seg_ends, decay_all, state_add, end_zero, started = local_terms(
        x_heads, b_proj, c_proj, dt_vals, flag_vals, init_vals, decay_rate[0]
    )
    seq_count = lax.axis_size("seq")
    seq_at = lax.axis_index("seq")
    heads_n, p_n, n_n = state_add.shape
    ones = jnp.ones((heads_n,), jnp.float32)
    zeros_state = jnp.zeros_like(state_add)
    has_start = jnp.where(started > 0, 1.0, 0.0).astype(jnp.float32)

    def pack(decay, state, mark):
        aux = jnp.concatenate(
            [
                jnp.broadcast_to(decay[:, None], (heads_n, n_n // 2)),
                jnp.broadcast_to(mark, (heads_n, n_n - n_n // 2)),
            ],
            axis=1,
        )
        return jnp.concatenate([state, aux[:, None, :]], axis=1)

    def unpack(packed):
        return (packed[:, p_n, 0], packed[:, :p_n], packed[0, p_n, n_n - 1])

    fwd_in = (decay_all * ones, state_add)
    fwd_ex = (ones, zeros_state)
    bwd_in = (jnp.exp(end_zero), seg_ends[0], has_start)
    bwd_ex = (ones, zeros_state, jnp.zeros((), jnp.float32))
    shift = 1
    while shift < seq_count:
        last = 2 * shift >= seq_count
        got_f = from_behind(pack(fwd_in[0], fwd_in[1], 0.0), "seq", shift)
        got_b = from_behind(pack(*bwd_in), "seq", -shift)
        early_a, early_b, _ = unpack(got_f)
        late_a, late_b, late_m = unpack(got_b)
        late_ok = seq_at + shift < seq_count
        fwd_ex = (fwd_ex[0] * early_a, fwd_ex[0][:, None, None] * early_b + fwd_ex[1])

        def near_far(near, far_a, far_b, far_m):
            keep = (near[2] > 0.5) | jnp.logical_not(late_ok)
            return (
                jnp.where(keep, near[0], far_a * near[0]),
                jnp.where(keep, near[1], far_a[:, None, None] * near[1] + far_b),
                jnp.where(keep, near[2], far_m),
            )

        bwd_ex = near_far(bwd_ex, late_a, late_b, late_m)
        if not last:
            fwd_in = (fwd_in[0] * early_a, fwd_in[0][:, None, None] * early_b + fwd_in[1])
            bwd_in = near_far(bwd_in, late_a, late_b, late_m)
        shift *= 2
    state_in = fwd_ex[1]
    carried_in = jnp.einsum("tn,hpn->thp", c_proj.astype(jnp.float32), state_in, precision=PRECISE)
    y_full = (
        y_part
        + carried[:, :, None] * carried_in
        + d_skip[0][None, :, None] * x_heads.astype(jnp.float32)
    )
    tail_state = bwd_ex[0][:, None, None] * state_add + bwd_ex[1]
    slot_ids = jnp.arange(1, init_vals.shape[0] + 1, dtype=jnp.int32)
    finals = jnp.where(
        (slot_ids < started)[:, None, None, None],
        seg_ends[1:],
        jnp.where((slot_ids == started)[:, None, None, None], tail_state[None], 0.0),
    )
    gated = y_full.reshape(rows_here, channels) * jax.nn.silu(z_gate.astype(jnp.float32))
    partial_sq = jnp.sum(gated * gated, axis=-1)
    total_sq = lax.psum(partial_sq, "row")
    mean_sq = total_sq / (channels * lax.axis_size("row"))
    gated_out = (gated * lax.rsqrt(mean_sq + EPSILON)[:, None] * norm_gain[0][None, :]).astype(
        jnp.bfloat16
    )
    return (gated_out.reshape(rows_here, 1, channels), finals[:, None])


def solution(mesh):
    placed = (
        P(("seq", "row"), "col"),
        P("col", None, "row"),
        P("col", None, "row"),
        P("col", None, None),
        P("col", None, "row"),
        P(None, "col", "row"),
        P(None, "col", None),
        P("col", "row"),
        P("col", None),
        P("col", "row"),
        P("col", "row"),
        P("col", "row"),
        P("col", "row"),
        P("seq"),
        P("seq", "col", "row", None, None),
        P("seq", None, "col", "row"),
        P("seq", None, "col", None),
    )
    return jax.shard_map(
        shards,
        mesh=mesh,
        in_specs=placed,
        out_specs=(P("seq", "col", "row"), P("seq", "col", "row", None, None)),
        check_vma=False,
    )
```

profile of v0, /device:TPU:101, one launch (start us, length us, event | category | flops | bytes accessed | tf_op | source)
XLA Modules:
  0.0 338.3 jit_solution(753345638524201628)
XLA Ops:
  8.0 18.5 %all-gather.2.cloned.1.call-done = bf16[512,1024]{1,0:T(8,128)(2,1)} async-done(((bf16[256,1024]{1,0:T(8,128)(2,1)}), bf16[512,1024]{1,0:T(8,128)(2,1)}) %all-gather.2.cloned.1.call-update) | async-done | bytes 1048592 | tf_op jit(solution)/shard_map/all_gather | solution.py:118
  26.5 1.6 convolution_bitcast_fusion
  28.1 3.3 fusion.30
  31.6 2.7 fusion.23
  34.3 2.7 fusion.20
  37.0 4.4 %pad_maximum_fusion = f32[4,512,1288]{1,2,0:T(8,128)} fusion(f32[4,512,8]{1,2,0:T(8,128)S(1)} %convolution_bitcast_fusion, f32[4,512,256]{1,2,0:T(8,128)S(1)} %fusion.30, f32[4,512,512]{1,2,0:T(8,128)S(1)} %fusion.23, f32[4,512,512]{1,2,0:T(8,128)S(1)} %fusion.20), kind=kLoop, calls=%fused_computation.5 | loop fusion | flops 7913472 | bytes 21102592 | tf_op jit(solution)/shard_map/concatenate | solution.py:128
  54.0 1.2 add_compare_fusion
  55.2 1.2 broadcast_compare_fusion.5
  56.4 1.2 iota_compare_fusion.16
  57.6 1.3 broadcast_compare_fusion.3
  64.6 0.9 fusion.50
  65.5 1.1 fusion.71
  66.7 1.1 fusion.73
  68.7 74.4 %reduce-scatter.2.cloned.1.call-done = f32[1,512,1288]{1,2,0:T(8,128)} async-done(((f32[4,512,1288]{1,2,0:T(8,128)}), f32[1,512,1288]{1,2,0:T(8,128)}) %reduce-scatter.2.cloned.1.call-update) | async-done | bytes 2637840 | tf_op jit(solution)/shard_map/reduce_scatter | solution.py:127
  143.1 1.9 convert_bitcast_fusion
  145.0 1.7 slice_select_fusion
  146.6 4.4 %collective-permute-start = (bf16[3,512]{0,1:T(8,128)(2,1)}, bf16[3,512]{0,1:T(8,128)(2,1)}, u32[]{:S(2)}, u32[]{:S(2)}) collective-permute-start(bf16[3,512]{0,1:T(8,128)(2,1)} %slice_select_fusion), channel_id=1, source_target_pairs={{0,8},{8,16},{16,24},{24,32},{32,40},{40,48},{48,56},{56,64},{64,7... | collective-permute-start | bytes 9224 | tf_op jit(solution)/shard_map/ppermute | solution.py:15
  151.7 2.5 collective-permute-start.1
  154.2 1.4 compare_select_fusion
  155.6 1.1 reduce-window.60
  156.9 1.3 exponential_select_fusion
  159.0 1.6 gather_fusion.3
  162.3 2.0 multiply_convert_fusion.2
  164.3 2.5 multiply_convert_fusion.1
  167.0 2.2 fusion.11
  169.9 3.0 collective-permute-start.7
  174.6 5.7 %collective-permute-done.7 = f32[8,65,128]{2,1,0:T(8,128)S(1)} collective-permute-done((f32[8,65,128]{2,1,0:T(8,128)S(1)}, f32[8,65,128]{2,1,0:T(8,128)S(1)}, u32[]{:S(2)}, u32[]{:S(2)}) %collective-permute-start.7) | collective-permute-done | bytes 266272 | tf_op jit(solution)/shard_map/ppermute | solution.py:15
  183.1 1.9 collective-permute-start.8
  185.7 1.0 gather_fusion.2
  187.5 1.3 subtract_exponential_fusion
  188.8 12.3 %collective-permute-done.8 = f32[8,65,128]{2,1,0:T(8,128)} collective-permute-done((f32[8,65,128]{2,1,0:T(8,128)}, f32[8,65,128]{2,1,0:T(8,128)}, u32[]{:S(2)}, u32[]{:S(2)}) %collective-permute-start.8) | collective-permute-done | bytes 266272 | tf_op jit(solution)/shard_map/ppermute | solution.py:15
  201.1 0.9 slice_reduce_fusion.4
  202.7 1.3 slice.312
  204.8 1.1 add_select_fusion.2
  206.6 4.4 %collective-permute-start.9 = (f32[8,65,128]{2,1,0:T(8,128)}, f32[8,65,128]{2,1,0:T(8,128)}, u32[]{:S(2)}, u32[]{:S(2)}) collective-permute-start(f32[8,65,128]{2,1,0:T(8,128)} %pad_maximum_fusion.9), channel_id=1, source_target_pairs={{32,0},{40,8},{48,16},{56,24},{64,32},{72,40},{80,48},{88,56},{96,... | collective-permute-start | bytes 798728 | tf_op jit(solution)/shard_map/ppermute | solution.py:15
  211.0 1.4 slice_add_fusion
  212.4 15.0 %collective-permute-done.9 = f32[8,65,128]{2,1,0:T(8,128)} collective-permute-done((f32[8,65,128]{2,1,0:T(8,128)}, f32[8,65,128]{2,1,0:T(8,128)}, u32[]{:S(2)}, u32[]{:S(2)}) %collective-permute-start.9) | collective-permute-done | bytes 266272 | tf_op jit(solution)/shard_map/ppermute | solution.py:15
  227.4 0.9 slice_reduce_fusion.3
  229.0 1.3 slice.315
  230.9 1.1 add_select_fusion.1
  232.7 1.9 collective-permute-start.10
  234.6 1.1 fusion.45
  236.5 1.9 collective-permute-start.2
  238.4 4.0 %collective-permute-done.10 = f32[8,65,128]{2,1,0:T(8,128)} collective-permute-done((f32[8,65,128]{2,1,0:T(8,128)}, f32[8,65,128]{2,1,0:T(8,128)}, u32[]{:S(2)}, u32[]{:S(2)}) %collective-permute-start.10) | collective-permute-done | bytes 266272 | tf_op jit(solution)/shard_map/ppermute | solution.py:15
  243.3 1.3 slice.318
  245.2 1.1 add_select_fusion
  247.0 2.0 collective-permute-start.11
  250.3 0.9 fusion.111
  253.7 1.0 fusion.101
  254.7 1.6 fusion.60
  256.4 2.1 collective-permute-start.3
  258.5 2.3 fusion.51
  260.8 13.4 %collective-permute-done.3 = f32[8,65,128]{2,1,0:T(8,128)S(1)} collective-permute-done((f32[8,65,128]{2,1,0:T(8,128)S(1)}, f32[8,65,128]{2,1,0:T(8,128)S(1)}, u32[]{:S(2)}, u32[]{:S(2)}) %collective-permute-start.3) | collective-permute-done | bytes 266272 | tf_op jit(solution)/shard_map/ppermute | solution.py:15
  274.2 0.9 fusion.114
  275.4 3.2 collective-permute-start.4
  279.4 12.3 %collective-permute-done.4 = f32[8,65,128]{2,1,0:T(8,128)S(1)} collective-permute-done((f32[8,65,128]{2,1,0:T(8,128)S(1)}, f32[8,65,128]{2,1,0:T(8,128)S(1)}, u32[]{:S(2)}, u32[]{:S(2)}) %collective-permute-start.4) | collective-permute-done | bytes 266272 | tf_op jit(solution)/shard_map/ppermute | solution.py:15
  292.1 13.5 %collective-permute-start.5 = (f32[8,65,128]{2,1,0:T(8,128)S(1)}, f32[8,65,128]{2,1,0:T(8,128)S(1)}, u32[]{:S(2)}, u32[]{:S(2)}) collective-permute-start(f32[8,65,128]{2,1,0:T(8,128)S(1)} %pad_maximum_fusion.5), channel_id=1, source_target_pairs={{0,64},{8,72},{16,80},{24,88},{32,96},{40,104},{48,112},{56,120},{... | collective-permute-start | bytes 798728 | tf_op jit(solution)/shard_map/ppermute | solution.py:15
  305.8 6.9 %fusion.38 = f32[512,8,64]{0,2,1:T(8,128)S(1)} fusion(bf16[512,8,64]{0,2,1:T(8,128)(2,1)S(1)} %bitcast.150, f32[8,512]{1,0:T(8,128)S(1)} %copy-done.18, f32[512,512]{1,0:T(8,128)S(1)} %fusion.93, f32[8,512]{1,0:T(8,128)S(1)} %copy-done.20, pred[512,512]{1,0:T(8,128)(4,1)S(1)} %copy-done.8, f32[512,8,64]{0,2,1:T(8,128)S(1)} %bitcast.152, ...), kind=kOutput, calls=%fused_computation.38 | convolution fusion | flops 1621622784 | bytes 3981312 | tf_op jit(solution)/shard_map/hij,jhp->ihp/dot_general | solution.py:36
  313.0 1.3 collective-permute-start.6
  314.3 1.0 select_bitcast_fusion
  315.4 8.0 %collective-permute-done.6 = f32[8,65,128]{2,1,0:T(8,128)S(1)} collective-permute-done((f32[8,65,128]{2,1,0:T(8,128)S(1)}, f32[8,65,128]{2,1,0:T(8,128)S(1)}, u32[]{:S(2)}, u32[]{:S(2)}) %collective-permute-start.6) | collective-permute-done | bytes 266272 | tf_op jit(solution)/shard_map/ppermute | solution.py:15
  323.4 1.7 fusion.37
  325.5 4.6 %psum.7 = f32[512]{0:T(512)S(1)} all-reduce(f32[512]{0:T(512)S(1)} %multiply_reduce_fusion), channel_id=1, replica_groups=mesh['seq'=32,'row'=2,'col'=4] {'row'}, use_global_device_ids=true, to_apply=%region_15.16 | all-reduce | flops 512 | bytes 4096 | tf_op jit(solution)/shard_map/psum | solution.py:239
  330.4 1.0 copy.69
  (224 shorter events, 36.0 us)
Async XLA Ops:
  7.2 19.3 %copy-start = (bf16[1024,4,8]{0,2,1:T(8,128)(2,1)S(1)}, bf16[1024,4,8]{0,2,1:T(8,128)(2,1)}, u32[]{:S(2)}) copy-start(bf16[1024,4,8]{0,2,1:T(8,128)(2,1)} %param.21) | copy-start | bytes 196612
  7.2 19.3 %all-gather.2.cloned.1.call-start = ((), (), s32[]{:S(2)}) async-start(), calls=%async_computation.1 | async-start | bytes 1572864 | tf_op jit(solution)/shard_map/all_gather | solution.py:118
  7.9 135.1 %reduce-scatter.2.cloned.1.call-start = ((), (), s32[]{:S(2)}) async-start(), calls=%async_computation.2 | async-start | bytes 13189120 | tf_op jit(solution)/shard_map/reduce_scatter | solution.py:127
  28.1 3.3 copy-start.6
  28.1 3.5 %copy-start.44 = (bf16[1024,4,512]{2,1,0:T(4,128)(2,1)S(1)}, bf16[1024,4,512]{2,1,0:T(4,128)(2,1)}, u32[]{:S(2)}) copy-start(bf16[1024,4,512]{2,1,0:T(4,128)(2,1)} %param.19) | copy-start | bytes 12582916
  31.6 2.7 copy-start.45
  41.4 0.7 copy-start.23
  41.4 3.8 %copy-start.9 = (bf16[3,3,1,512]{3,1,2,0:T(4,128)(2,1)S(1)}, bf16[3,3,1,512]{3,1,2,0:T(4,128)(2,1)}, u32[]{:S(2)}) copy-start(bf16[3,3,1,512]{3,1,2,0:T(4,128)(2,1)} %param.32) | copy-start | bytes 27652
  41.4 9.4 %copy-start.32 = (bf16[1,512]{1,0:T(2,128)(2,1)S(1)}, bf16[1,512]{1,0:T(2,128)(2,1)}, u32[]{:S(2)}) copy-start(bf16[1,512]{1,0:T(2,128)(2,1)} %param.24) | copy-start | bytes 3076
  41.4 10.0 %copy-start.11 = (bf16[3,3,1,256]{3,1,2,0:T(4,128)(2,1)S(1)}, bf16[3,3,1,256]{3,1,2,0:T(4,128)(2,1)}, u32[]{:S(2)}) copy-start(bf16[3,3,1,256]{3,1,2,0:T(4,128)(2,1)} %param.33) | copy-start | bytes 13828
  41.4 10.7 %copy-start.37 = (bf16[1,256]{1,0:T(2,128)(2,1)S(1)}, bf16[1,256]{1,0:T(2,128)(2,1)}, u32[]{:S(2)}) copy-start(bf16[1,256]{1,0:T(2,128)(2,1)} %param.25) | copy-start | bytes 1540
  41.4 21.9 %copy-start.24 = (bf16[4,1,256]{2,0,1:T(4,128)(2,1)S(1)}, bf16[4,1,256]{2,0,1:T(4,128)(2,1)}, u32[]{:S(2)}) copy-start(bf16[4,1,256]{2,0,1:T(4,128)(2,1)} %param.23) | copy-start | bytes 6148
  41.5 22.6 %copy-start.21 = (bf16[4,1,512]{2,0,1:T(4,128)(2,1)S(1)}, bf16[4,1,512]{2,0,1:T(4,128)(2,1)}, u32[]{:S(2)}) copy-start(bf16[4,1,512]{2,0,1:T(4,128)(2,1)} %param.22) | copy-start | bytes 12292
  45.3 23.4 %copy-start.10 = (bf16[9,512]{1,0:T(8,128)(2,1)}, bf16[9,512]{1,0:T(8,128)(2,1)S(1)}, u32[]{:S(2)}) copy-start(bf16[9,512]{1,0:T(8,128)(2,1)S(1)} %reshape_squeeze.6) | copy-start | bytes 27652
  143.1 8.0 %copy-start.30 = (pred[3]{0:T(512)(128)(4,1)S(1)}, pred[3]{0:T(512)(128)(4,1)}, u32[]{:S(2)}) copy-start(pred[3]{0:T(512)(128)(4,1)} %add_compare_fusion) | copy-start | bytes 13
  146.6 17.6 %collective-permute-start = (bf16[3,512]{0,1:T(8,128)(2,1)}, bf16[3,512]{0,1:T(8,128)(2,1)}, u32[]{:S(2)}, u32[]{:S(2)}) collective-permute-start(bf16[3,512]{0,1:T(8,128)(2,1)} %slice_select_fusion), channel_id=1, source_target_pairs={{0,8},{8,16},{16,24},{24,32},{32,40},{40,48},{48,56},{56,64},{64,7... | collective-permute-start | bytes 9224 | tf_op jit(solution)/shard_map/ppermute | solution.py:15
  151.7 10.5 %collective-permute-start.1 = (bf16[3,256]{0,1:T(8,128)(2,1)}, bf16[3,256]{0,1:T(8,128)(2,1)}, u32[]{:S(2)}, u32[]{:S(2)}) collective-permute-start(bf16[3,256]{0,1:T(8,128)(2,1)} %slice_select_fusion.1), channel_id=1, source_target_pairs={{0,8},{8,16},{16,24},{24,32},{32,40},{40,48},{48,56},{56,64},{64,7... | collective-permute-start | bytes 4616 | tf_op jit(solution)/shard_map/ppermute | solution.py:15
  156.9 2.1 copy-start.16
  161.4 5.4 %copy-start.14 = (f32[4,8]{1,0:T(4,128)}, f32[4,8]{1,0:T(4,128)S(1)}, u32[]{:S(2)}) copy-start(f32[4,8]{1,0:T(4,128)S(1)} %broadcast_select_fusion.5) | copy-start | bytes 388
  164.3 8.7 %copy-start.4 = (bf16[512,256]{0,1:T(8,128)(2,1)}, bf16[512,256]{0,1:T(8,128)(2,1)S(1)}, u32[]{:S(2)}) copy-start(bf16[512,256]{0,1:T(8,128)(2,1)S(1)} %multiply_convert_fusion.2) | copy-start | bytes 786436
  166.8 6.1 %copy-start.2 = (bf16[512,512]{0,1:T(8,128)(2,1)}, bf16[512,512]{0,1:T(8,128)(2,1)S(1)}, u32[]{:S(2)}) copy-start(bf16[512,512]{0,1:T(8,128)(2,1)S(1)} %multiply_convert_fusion.1) | copy-start | bytes 1572868
  166.8 6.1 %copy-start.28 = (f32[1,8]{1,0:T(1,128)S(1)}, f32[1,8]{1,0:T(1,128)}, u32[]{:S(2)}) copy-start(f32[1,8]{1,0:T(1,128)} %param.26) | copy-start | bytes 100
  166.8 6.1 %copy-start.29 = (f32[1,8]{1,0:T(1,128)S(1)}, f32[1,8]{1,0:T(1,128)}, u32[]{:S(2)}) copy-start(f32[1,8]{1,0:T(1,128)} %param.27) | copy-start | bytes 100
  166.8 18.2 %copy-start.31 = (pred[3]{0:T(512)(128)(4,1)S(1)}, pred[3]{0:T(512)(128)(4,1)}, u32[]{:S(2)}) copy-start(pred[3]{0:T(512)(128)(4,1)} %broadcast_compare_fusion.5) | copy-start | bytes 13
  166.8 18.8 %copy-start.22 = (s32[1024]{0:T(1024)S(1)}, s32[1024]{0:T(1024)}, u32[]{:S(2)}) copy-start(s32[1024]{0:T(1024)} %pad_clamp_fusion.2) | copy-start | bytes 12292
  166.8 13.6 %copy-start.15 = (f32[4,8]{1,0:T(4,128)S(1)}, f32[4,8]{1,0:T(4,128)}, u32[]{:S(2)}) copy-start(f32[4,8]{1,0:T(4,128)} %copy-done.14) | copy-start | bytes 388
  169.9 10.4 %collective-permute-start.7 = (f32[8,65,128]{2,1,0:T(8,128)S(1)}, f32[8,65,128]{2,1,0:T(8,128)S(1)}, u32[]{:S(2)}, u32[]{:S(2)}) collective-permute-start(f32[8,65,128]{2,1,0:T(8,128)S(1)} %pad_maximum_fusion.7), channel_id=1, source_target_pairs={{8,0},{16,8},{24,16},{32,24},{40,32},{48,40},{56,48},{64,56},{72,6... | collective-permute-start | bytes 798728 | tf_op jit(solution)/shard_map/ppermute | solution.py:15
  180.3 24.5 %copy-start.7 = (f32[8,65,128]{2,1,0:T(8,128)}, f32[8,65,128]{2,1,0:T(8,128)S(1)}, u32[]{:S(2)}) copy-start(f32[8,65,128]{2,1,0:T(8,128)S(1)} %collective-permute-done.7) | copy-start | bytes 798724
  181.0 4.0 %copy-start.25 = (f32[8]{0:T(128)}, f32[8]{0:T(128)S(1)}, u32[]{:S(2)}) copy-start(f32[8]{0:T(128)S(1)} %get-tuple-element.55) | copy-start | bytes 100
  183.1 18.0 %collective-permute-start.8 = (f32[8,65,128]{2,1,0:T(8,128)}, f32[8,65,128]{2,1,0:T(8,128)}, u32[]{:S(2)}, u32[]{:S(2)}) collective-permute-start(f32[8,65,128]{2,1,0:T(8,128)} %pad_maximum_fusion.8), channel_id=1, source_target_pairs={{16,0},{24,8},{32,16},{40,24},{48,32},{56,40},{64,48},{72,56},{80,... | collective-permute-start | bytes 798728 | tf_op jit(solution)/shard_map/ppermute | solution.py:15
  188.8 60.3 %copy-start.17 = (f32[8,4]{0,1:T(4,128)S(1)}, f32[8,4]{0,1:T(4,128)}, u32[]{:S(2)}) copy-start(f32[8,4]{0,1:T(4,128)} %copy-done.16) | copy-start | bytes 388
  202.7 2.0 copy-start.26
  204.8 29.8 %copy-start.40 = (pred[4]{0:T(512)(128)(4,1)S(1)}, pred[4]{0:T(512)(128)(4,1)}, u32[]{:S(2)}) copy-start(pred[4]{0:T(512)(128)(4,1)} %iota_compare_fusion.16) | copy-start | bytes 16
  204.8 46.9 %copy-start.27 = (f32[8]{0:T(128)S(1)}, f32[8]{0:T(128)}, u32[]{:S(2)}) copy-start(f32[8]{0:T(128)} %get-tuple-element.21) | copy-start | bytes 100
  204.8 49.9 %copy-start.34 = (f32[8]{0:T(128)S(1)}, f32[8]{0:T(128)}, u32[]{:S(2)}) copy-start(f32[8]{0:T(128)} %get-tuple-element.54) | copy-start | bytes 100
  206.6 20.8 %collective-permute-start.9 = (f32[8,65,128]{2,1,0:T(8,128)}, f32[8,65,128]{2,1,0:T(8,128)}, u32[]{:S(2)}, u32[]{:S(2)}) collective-permute-start(f32[8,65,128]{2,1,0:T(8,128)} %pad_maximum_fusion.9), channel_id=1, source_target_pairs={{32,0},{40,8},{48,16},{56,24},{64,32},{72,40},{80,48},{88,56},{96,... | collective-permute-start | bytes 798728 | tf_op jit(solution)/shard_map/ppermute | solution.py:15
  212.4 46.1 %copy-start.1 = (f32[3,1,8,64,128]{4,3,2,1,0:T(8,128)S(1)}, f32[3,1,8,64,128]{4,3,2,1,0:T(8,128)}, u32[]{:S(2)}) copy-start(f32[3,1,8,64,128]{4,3,2,1,0:T(8,128)} %param.31) | copy-start | bytes 2359300
  232.7 9.7 %collective-permute-start.10 = (f32[8,65,128]{2,1,0:T(8,128)}, f32[8,65,128]{2,1,0:T(8,128)}, u32[]{:S(2)}, u32[]{:S(2)}) collective-permute-start(f32[8,65,128]{2,1,0:T(8,128)} %pad_maximum_fusion.10), channel_id=1, source_target_pairs={{64,0},{72,8},{80,16},{88,24},{96,32},{104,40},{112,48},{120,56},{... | collective-permute-start | bytes 798728 | tf_op jit(solution)/shard_map/ppermute | solution.py:15
  236.5 13.8 %collective-permute-start.2 = (f32[8,65,128]{2,1,0:T(8,128)}, f32[8,65,128]{2,1,0:T(8,128)}, u32[]{:S(2)}, u32[]{:S(2)}) collective-permute-start(f32[8,65,128]{2,1,0:T(8,128)} %pad_maximum_fusion.2), channel_id=1, source_target_pairs={{0,8},{8,16},{16,24},{24,32},{32,40},{40,48},{48,56},{56,64},{64,7... | collective-permute-start | bytes 798728 | tf_op jit(solution)/shard_map/ppermute | solution.py:15
  247.0 6.6 %collective-permute-start.11 = (f32[8,65,128]{2,1,0:T(8,128)}, f32[8,65,128]{2,1,0:T(8,128)}, u32[]{:S(2)}, u32[]{:S(2)}) collective-permute-start(f32[8,65,128]{2,1,0:T(8,128)} %pad_maximum_fusion.11), channel_id=1, source_target_pairs={{128,0},{136,8},{144,16},{152,24},{160,32},{168,40},{176,48},{184,... | collective-permute-start | bytes 798728 | tf_op jit(solution)/shard_map/ppermute | solution.py:15
  251.2 0.5 copy-start.35
  251.7 3.0 copy-start.41
  254.7 20.5 %copy-start.42 = (f32[8]{0:T(128)S(1)}, f32[8]{0:T(128)}, u32[]{:S(2)}) copy-start(f32[8]{0:T(128)} %copy-done.41) | copy-start | bytes 100
  254.7 23.9 %copy-start.13 = (f32[512,3]{0,1:T(4,128)S(1)}, f32[512,3]{0,1:T(4,128)}, u32[]{:S(2)}) copy-start(f32[512,3]{0,1:T(4,128)} %copy.86) | copy-start | bytes 18436
  256.4 22.7 %copy-start.5 = (bf16[512,256]{0,1:T(8,128)(2,1)S(1)}, bf16[512,256]{0,1:T(8,128)(2,1)}, u32[]{:S(2)}) copy-start(bf16[512,256]{0,1:T(8,128)(2,1)} %copy-done.4) | copy-start | bytes 786436
  256.4 17.8 %collective-permute-start.3 = (f32[8,65,128]{2,1,0:T(8,128)S(1)}, f32[8,65,128]{2,1,0:T(8,128)S(1)}, u32[]{:S(2)}, u32[]{:S(2)}) collective-permute-start(f32[8,65,128]{2,1,0:T(8,128)S(1)} %pad_maximum_fusion.3), channel_id=1, source_target_pairs={{0,16},{8,24},{16,32},{24,40},{32,48},{40,56},{48,64},{56,72},{64,... | collective-permute-start | bytes 798728 | tf_op jit(solution)/shard_map/ppermute | solution.py:15
  260.8 44.9 %copy-start.3 = (bf16[512,512]{0,1:T(8,128)(2,1)S(1)}, bf16[512,512]{0,1:T(8,128)(2,1)}, u32[]{:S(2)}) copy-start(bf16[512,512]{0,1:T(8,128)(2,1)} %copy-done.2) | copy-start | bytes 1572868
  260.8 44.9 %copy-start.8 = (pred[512,512]{1,0:T(8,128)(4,1)S(1)}, pred[512,512]{1,0:T(8,128)(4,1)}, u32[]{:S(2)}) copy-start(pred[512,512]{1,0:T(8,128)(4,1)} %fusion.50) | copy-start | bytes 786436
  260.8 44.9 %copy-start.18 = (f32[8,512]{1,0:T(8,128)S(1)}, f32[8,512]{1,0:T(8,128)}, u32[]{:S(2)}) copy-start(f32[8,512]{1,0:T(8,128)} %get-tuple-element.34) | copy-start | bytes 49156
  260.8 44.9 %copy-start.19 = (f32[512,8]{0,1:T(8,128)S(1)}, f32[512,8]{0,1:T(8,128)}, u32[]{:S(2)}) copy-start(f32[512,8]{0,1:T(8,128)} %subtract_exponential_fusion) | copy-start | bytes 49156
  260.8 44.9 %copy-start.20 = (f32[8,512]{1,0:T(8,128)S(1)}, f32[8,512]{1,0:T(8,128)}, u32[]{:S(2)}) copy-start(f32[8,512]{1,0:T(8,128)} %add_bitcast_fusion.1) | copy-start | bytes 49156
  275.4 16.4 %collective-permute-start.4 = (f32[8,65,128]{2,1,0:T(8,128)S(1)}, f32[8,65,128]{2,1,0:T(8,128)S(1)}, u32[]{:S(2)}, u32[]{:S(2)}) collective-permute-start(f32[8,65,128]{2,1,0:T(8,128)S(1)} %pad_maximum_fusion.4), channel_id=1, source_target_pairs={{0,32},{8,40},{16,48},{24,56},{32,64},{40,72},{48,80},{56,88},{64,... | collective-permute-start | bytes 798728 | tf_op jit(solution)/shard_map/ppermute | solution.py:15
  292.1 20.5 %collective-permute-start.5 = (f32[8,65,128]{2,1,0:T(8,128)S(1)}, f32[8,65,128]{2,1,0:T(8,128)S(1)}, u32[]{:S(2)}, u32[]{:S(2)}) collective-permute-start(f32[8,65,128]{2,1,0:T(8,128)S(1)} %pad_maximum_fusion.5), channel_id=1, source_target_pairs={{0,64},{8,72},{16,80},{24,88},{32,96},{40,104},{48,112},{56,120},{... | collective-permute-start | bytes 798728 | tf_op jit(solution)/shard_map/ppermute | solution.py:15
  305.7 8.6 %copy-start.38 = (pred[3]{0:T(512)(128)(4,1)S(1)}, pred[3]{0:T(512)(128)(4,1)}, u32[]{:S(2)}) copy-start(pred[3]{0:T(512)(128)(4,1)} %get-tuple-element.58) | copy-start | bytes 13
  305.7 8.6 %copy-start.39 = (pred[3]{0:T(512)(128)(4,1)S(1)}, pred[3]{0:T(512)(128)(4,1)}, u32[]{:S(2)}) copy-start(pred[3]{0:T(512)(128)(4,1)} %get-tuple-element.59) | copy-start | bytes 13
  305.7 17.7 %copy-start.12 = (f32[512,8]{0,1:T(8,128)S(1)}, f32[512,8]{0,1:T(8,128)}, u32[]{:S(2)}) copy-start(f32[512,8]{0,1:T(8,128)} %get-tuple-element.23) | copy-start | bytes 49156
  305.7 17.7 %copy-start.36 = (f32[8]{0:T(128)S(1)}, f32[8]{0:T(128)}, u32[]{:S(2)}) copy-start(f32[8]{0:T(128)} %copy-done.35) | copy-start | bytes 100
  305.7 17.7 %copy-start.43 = (f32[1,8]{1,0:T(1,128)S(1)}, f32[1,8]{1,0:T(1,128)}, u32[]{:S(2)}) copy-start(f32[1,8]{1,0:T(1,128)} %param.28) | copy-start | bytes 100
  313.0 17.1 %copy-start.33 = (f32[1,512]{1,0:T(1,128)S(1)}, f32[1,512]{1,0:T(1,128)}, u32[]{:S(2)}) copy-start(f32[1,512]{1,0:T(1,128)} %param.29) | copy-start | bytes 6148
  313.0 10.4 %collective-permute-start.6 = (f32[8,65,128]{2,1,0:T(8,128)S(1)}, f32[8,65,128]{2,1,0:T(8,128)S(1)}, u32[]{:S(2)}, u32[]{:S(2)}) collective-permute-start(f32[8,65,128]{2,1,0:T(8,128)S(1)} %pad_maximum_fusion.6), channel_id=1, source_target_pairs={{0,128},{8,136},{16,144},{24,152},{32,160},{40,168},{48,176},{56,1... | collective-permute-start | bytes 798728 | tf_op jit(solution)/shard_map/ppermute | solution.py:15
Sparse Core Ops, SparseCore 0:
  9.8 16.6 all-gather.1
  41.6 101.4 reduce-scatter.1
where the time goes:
time: 340 us; the launch traced here: 338 us
  waiting for transfers between devices  164 us (48%)
  other arithmetic  51.4 us (15%)
  starting transfers between devices  42.1 us (12%)
  matrix products  31.3 us (9%)
  between operations  22.6 us (7%)
  local copies, waits for them, and re-layouts  22 us (6%)
  blocking collectives  4.56 us (1%)
    reduce_scatter x1, waiting for transfers between devices, shards(): lax.psum_scatter(jnp.concatenate(pieces, axis=2), 'col', scatter_dimensio...  74.4 us
    ppermute x12, waiting for transfers between devices, from_behind(): lax.ppermute(value, axis, [(source, source + steps) for source in range(f...  70.8 us
    ppermute x12, starting transfers between devices, from_behind(): lax.ppermute(value, axis, [(source, source + steps) for source in range(f...  42 us
    all_gather x1, waiting for transfers between devices, shards(): tokens = lax.all_gather(hidden, 'row', axis=0, tiled=True)  18.5 us
    dot_general x4, matrix products, shards(): jnp.einsum('td,dgc->gtc', tokens, weight, preferred_element_type=jnp.floa...  10.4 us
    dot_general x6, matrix products, convolve(): from_edge = jnp.dot(picker, table, preferred_element_type=jnp.float32)  7.59 us
    slice x9, local copies, waits for them, and re-layouts, unpack(): return (packed[:, p_n, 0], packed[:, :p_n], packed[0, p_n, n_n - 1])  7.41 us
    dot_general x1, matrix products, local_terms(): jnp.einsum('hij,jhp->ihp', mixing, x_vals.astype(jnp.float32), precision=...  6.86 us
  transfers between devices with their start and end apart: 14, of which 9 were waited for; matrix products, arithmetic and copies ran while one was open for 18% of the time, Pallas kernels for 0%

commit v1 on v0

--- a/solution.py
+++ b/solution.py
@@ -115,7 +115,9 @@
     conv_x_edges,
     conv_bc_edges,
 ):
-    tokens = lax.all_gather(hidden, "row", axis=0, tiled=True)
+    tokens = jnp.concatenate(
+        lax.all_to_all(jnp.stack([hidden] * lax.axis_size("row")), "row", 0, 0), axis=0
+    )
     rows_here = tokens.shape[0]
     channels = w_x.shape[2]
     heads_here = w_dt.shape[2]

time: 340 us -> 318 us (0.935)
  waiting for transfers between devices: 164 us -> 156 us
  other arithmetic: 51.4 us -> 44.9 us
  starting transfers between devices: 42.1 us -> 35.7 us
  blocking collectives: 4.56 us -> 9.6 us
  matrix products: 31.3 us -> 26.3 us
    all_gather x1 -> x0, waiting for transfers between devices: 18.5 us -> none  [shards(): tokens = lax.all_gather(hidden, 'row', axis=0, tiled=True)]
    ppermute x12, waiting for transfers between devices: 70.8 us -> 79.5 us  [from_behind(): lax.ppermute(value, axis, [(source, source + steps) for source in range(f...]
    ppermute x12, starting transfers between devices: 42 us -> 35.7 us  [from_behind(): lax.ppermute(value, axis, [(source, source + steps) for source in range(f...]
    all_to_all x0 -> x1, blocking collectives: none -> 4.88 us  [shards(): lax.all_to_all(jnp.stack([hidden] * lax.axis_size('row')), 'row', 0, 0)]
    dot_general x4 -> x3, matrix products: 10.4 us -> 6.49 us  [shards(): jnp.einsum('td,dgc->gtc', tokens, weight, preferred_element_type=jnp.floa...]
  transfers between devices with their start and end apart: 14 -> 13, of which waited for: 9 -> 9; matrix products, arithmetic and copies ran while one was open for 18% -> 15% of each run, Pallas kernels for 0% -> 0%
where the time goes in v1:
time: 318 us; the launch traced here: 315 us
  waiting for transfers between devices  156 us (49%)
  other arithmetic  44.9 us (14%)
  starting transfers between devices  35.7 us (11%)
  matrix products  26.3 us (8%)
  between operations  23 us (7%)
  local copies, waits for them, and re-layouts  19.2 us (6%)
  blocking collectives  9.6 us (3%)
    ppermute x12, waiting for transfers between devices, from_behind(): lax.ppermute(value, axis, [(source, source + steps) for source in range(f...  79.5 us
    reduce_scatter x1, waiting for transfers between devices, shards(): lax.psum_scatter(jnp.concatenate(pieces, axis=2), 'col', scatter_dimensio...  76.6 us
    ppermute x12, starting transfers between devices, from_behind(): lax.ppermute(value, axis, [(source, source + steps) for source in range(f...  35.7 us
    dot_general x6, matrix products, convolve(): from_edge = jnp.dot(picker, table, preferred_element_type=jnp.float32)  7.71 us
    dot_general x1, matrix products, local_terms(): jnp.einsum('hij,jhp->ihp', mixing, x_vals.astype(jnp.float32), precision=...  7.06 us
    dot_general x3, matrix products, shards(): jnp.einsum('td,dgc->gtc', tokens, weight, preferred_element_type=jnp.floa...  6.49 us
  transfers between devices with their start and end apart: 13, of which 9 were waited for; matrix products, arithmetic and copies ran while one was open for 15% of the time, Pallas kernels for 0%

profile of v1, /device:TPU:101, one launch (start us, length us, event | category | flops | bytes accessed | tf_op | source)
XLA Modules:
  0.0 314.9 jit_solution(6403444459835059835)
XLA Ops:
  7.2 1.4 pad_maximum_fusion.1
  8.7 4.9 %all_to_all.5 = bf16[2,256,1024]{2,1,0:T(8,128)(2,1)S(1)} all-to-all(bf16[2,256,1024]{2,1,0:T(8,128)(2,1)S(1)} %pad_maximum_fusion.1), channel_id=1, replica_groups=mesh['seq'=32,'row'=2,'col'=4] {'row'}, dimensions={0} | all-to-all | bytes 2097152 | tf_op jit(solution)/shard_map/all_to_all | solution.py:119
  13.5 1.3 fusion.30
  14.9 0.9 copy-done.45
  15.7 2.6 fusion.23
  18.4 2.6 fusion.20
  21.4 4.4 %pad_maximum_fusion = f32[4,512,1288]{1,2,0:T(8,128)} fusion(f32[4,512,8]{1,2,0:T(8,128)S(1)} %convolution_bitcast_fusion, f32[4,512,256]{1,2,0:T(8,128)S(1)} %fusion.30, f32[4,512,512]{1,2,0:T(8,128)S(1)} %fusion.23, f32[4,512,512]{1,2,0:T(8,128)S(1)} %fusion.20), kind=kLoop, calls=%fused_computation.5 | loop fusion | flops 7913472 | bytes 21102592 | tf_op jit(solution)/shard_map/concatenate | solution.py:130
  37.9 1.2 broadcast_compare_fusion.5
  39.1 1.2 iota_compare_fusion.16
  40.3 1.2 broadcast_compare_fusion.3
  47.3 0.9 fusion.46
  48.5 1.1 fusion.69
  50.1 1.4 fusion.70
  51.5 76.6 %reduce-scatter.2.cloned.1.call-done = f32[1,512,1288]{1,2,0:T(8,128)} async-done(((f32[4,512,1288]{1,2,0:T(8,128)}), f32[1,512,1288]{1,2,0:T(8,128)}) %reduce-scatter.2.cloned.1.call-update) | async-done | bytes 2637840 | tf_op jit(solution)/shard_map/reduce_scatter | solution.py:129
  128.1 1.9 convert_bitcast_fusion
  130.2 4.5 %collective-permute-start = (bf16[3,512]{0,1:T(8,128)(2,1)S(1)}, bf16[3,512]{0,1:T(8,128)(2,1)}, u32[]{:S(2)}, u32[]{:S(2)}) collective-permute-start(bf16[3,512]{0,1:T(8,128)(2,1)S(1)} %slice_select_fusion), channel_id=1, source_target_pairs={{0,8},{8,16},{16,24},{24,32},{32,40},{40,48},{48,56},{56,64},{64,7... | collective-permute-start | bytes 9224 | tf_op jit(solution)/shard_map/ppermute | solution.py:15
  135.5 2.5 collective-permute-start.1
  138.7 1.1 reduce-window.60
  141.5 0.7 broadcast_select_fusion.5
  143.2 1.8 multiply_convert_fusion.2
  145.0 2.6 multiply_convert_fusion.1
  147.8 2.1 fusion.11
  150.0 0.7 slice_bitcast_fusion
  151.5 2.9 collective-permute-start.7
  155.5 6.6 %collective-permute-done.7 = f32[8,65,128]{2,1,0:T(8,128)} collective-permute-done((f32[8,65,128]{2,1,0:T(8,128)}, f32[8,65,128]{2,1,0:T(8,128)}, u32[]{:S(2)}, u32[]{:S(2)}) %collective-permute-start.7) | collective-permute-done | bytes 266272 | tf_op jit(solution)/shard_map/ppermute | solution.py:15
  162.2 0.9 slice_reduce_fusion.5
  163.1 1.3 slice.309
  165.2 1.1 add_select_fusion.3
  166.3 0.7 pad_maximum_fusion.9
  167.0 1.9 collective-permute-start.8
  169.0 1.0 gather_fusion.2
  170.3 14.6 %collective-permute-done.8 = f32[8,65,128]{2,1,0:T(8,128)S(1)} collective-permute-done((f32[8,65,128]{2,1,0:T(8,128)}, f32[8,65,128]{2,1,0:T(8,128)S(1)}, u32[]{:S(2)}, u32[]{:S(2)}) %collective-permute-start.8) | collective-permute-done | bytes 266272 | tf_op jit(solution)/shard_map/ppermute | solution.py:15
  186.5 0.7 pad_maximum_fusion.10
  187.3 4.2 %collective-permute-start.9 = (f32[8,65,128]{2,1,0:T(8,128)}, f32[8,65,128]{2,1,0:T(8,128)}, u32[]{:S(2)}, u32[]{:S(2)}) collective-permute-start(f32[8,65,128]{2,1,0:T(8,128)} %pad_maximum_fusion.10), channel_id=1, source_target_pairs={{32,0},{40,8},{48,16},{56,24},{64,32},{72,40},{80,48},{88,56},{96,... | collective-permute-start | bytes 798728 | tf_op jit(solution)/shard_map/ppermute | solution.py:15
  191.5 1.3 slice_add_fusion
  192.9 15.3 %collective-permute-done.9 = f32[8,65,128]{2,1,0:T(8,128)} collective-permute-done((f32[8,65,128]{2,1,0:T(8,128)}, f32[8,65,128]{2,1,0:T(8,128)}, u32[]{:S(2)}, u32[]{:S(2)}) %collective-permute-start.9) | collective-permute-done | bytes 266272 | tf_op jit(solution)/shard_map/ppermute | solution.py:15
  208.2 0.9 slice_reduce_fusion.3
  209.1 1.3 slice.315
  211.1 1.1 add_select_fusion.1
  212.9 1.9 collective-permute-start.10
  214.8 1.1 fusion.45
  216.0 0.7 pad_maximum_fusion.3
  216.7 1.9 collective-permute-start.2
  218.6 4.0 %collective-permute-done.10 = f32[8,65,128]{2,1,0:T(8,128)S(1)} collective-permute-done((f32[8,65,128]{2,1,0:T(8,128)}, f32[8,65,128]{2,1,0:T(8,128)S(1)}, u32[]{:S(2)}, u32[]{:S(2)}) %collective-permute-start.10) | collective-permute-done | bytes 266272 | tf_op jit(solution)/shard_map/ppermute | solution.py:15
  224.3 0.7 pad_maximum_fusion.12
  225.1 2.0 collective-permute-start.11
  230.1 1.5 collective-permute-done.11
  231.6 0.9 fusion.98
  232.5 1.4 fusion.56
  233.9 1.9 collective-permute-start.3
  235.9 1.4 fusion.47
  237.3 14.7 %collective-permute-done.3 = f32[8,65,128]{2,1,0:T(8,128)S(1)} collective-permute-done((f32[8,65,128]{2,1,0:T(8,128)S(1)}, f32[8,65,128]{2,1,0:T(8,128)S(1)}, u32[]{:S(2)}, u32[]{:S(2)}) %collective-permute-start.3) | collective-permute-done | bytes 266272 | tf_op jit(solution)/shard_map/ppermute | solution.py:15
  252.4 3.0 collective-permute-start.4
  256.2 14.9 %collective-permute-done.4 = f32[8,65,128]{2,1,0:T(8,128)S(1)} collective-permute-done((f32[8,65,128]{2,1,0:T(8,128)S(1)}, f32[8,65,128]{2,1,0:T(8,128)S(1)}, u32[]{:S(2)}, u32[]{:S(2)}) %collective-permute-start.4) | collective-permute-done | bytes 266272 | tf_op jit(solution)/shard_map/ppermute | solution.py:15
  271.5 7.6 %collective-permute-start.5 = (f32[8,65,128]{2,1,0:T(8,128)S(1)}, f32[8,65,128]{2,1,0:T(8,128)S(1)}, u32[]{:S(2)}, u32[]{:S(2)}) collective-permute-start(f32[8,65,128]{2,1,0:T(8,128)S(1)} %pad_maximum_fusion.6), channel_id=1, source_target_pairs={{0,64},{8,72},{16,80},{24,88},{32,96},{40,104},{48,112},{56,120},{... | collective-permute-start | bytes 798728 | tf_op jit(solution)/shard_map/ppermute | solution.py:15
  279.1 7.1 %fusion.38 = f32[512,8,64]{0,2,1:T(8,128)S(1)} fusion(bf16[512,8,64]{0,2,1:T(8,128)(2,1)S(1)} %bitcast.157, f32[8,512]{1,0:T(8,128)S(1)} %copy-done.18, f32[512,512]{1,0:T(8,128)S(1)} %fusion.89, f32[8,512]{1,0:T(8,128)S(1)} %add_bitcast_fusion.1, pred[512,512]{1,0:T(8,128)(4,1)S(1)} %copy-done.10, f32[512,8,64]{0,2,1:T(8,128)S(1)} %bitcast.159, ...), kind=kOutput, calls=%fused_computation.38 | convolution fusion | flops 1621622784 | bytes 3981312 | tf_op jit(solution)/shard_map/hij,jhp->ihp/dot_general | solution.py:36
  286.6 1.3 collective-permute-start.6
  287.9 1.0 select_bitcast_fusion
  289.0 7.9 %collective-permute-done.6 = f32[8,65,128]{2,1,0:T(8,128)S(1)} collective-permute-done((f32[8,65,128]{2,1,0:T(8,128)S(1)}, f32[8,65,128]{2,1,0:T(8,128)S(1)}, u32[]{:S(2)}, u32[]{:S(2)}) %collective-permute-start.6) | collective-permute-done | bytes 266272 | tf_op jit(solution)/shard_map/ppermute | solution.py:15
  296.8 0.8 fusion.37
  297.6 1.4 multiply_reduce_fusion
  299.0 4.7 %psum.7 = f32[512]{0:T(512)S(1)} all-reduce(f32[512]{0:T(512)S(1)} %multiply_reduce_fusion), channel_id=1, replica_groups=mesh['seq'=32,'row'=2,'col'=4] {'row'}, use_global_device_ids=true, to_apply=%region_15.16 | all-reduce | flops 512 | bytes 4096 | tf_op jit(solution)/shard_map/psum | solution.py:241
  303.8 2.2 fusion.52
  306.0 2.0 copy.69
  (225 shorter events, 27.9 us)
Async XLA Ops:
  7.2 6.4 %copy-start = (bf16[1024,4,256]{2,1,0:T(4,128)(2,1)S(1)}, bf16[1024,4,256]{2,1,0:T(4,128)(2,1)}, u32[]{:S(2)}) copy-start(bf16[1024,4,256]{2,1,0:T(4,128)(2,1)} %param.20) | copy-start | bytes 6291460
  7.2 120.9 %reduce-scatter.2.cloned.1.call-start = ((), (), s32[]{:S(2)}) async-start(), calls=%async_computation.2 | async-start | bytes 13189120 | tf_op jit(solution)/shard_map/reduce_scatter | solution.py:129
  13.5 2.2 copy-start.45
  15.7 2.6 copy-start.46
  18.4 2.6 copy-start.14
  25.8 0.7 copy-start.21
  25.8 3.2 %copy-start.11 = (bf16[3,3,1,512]{3,1,2,0:T(4,128)(2,1)S(1)}, bf16[3,3,1,512]{3,1,2,0:T(4,128)(2,1)}, u32[]{:S(2)}) copy-start(bf16[3,3,1,512]{3,1,2,0:T(4,128)(2,1)} %param.32) | copy-start | bytes 27652
  25.8 8.2 %copy-start.29 = (bf16[1,512]{1,0:T(2,128)(2,1)S(1)}, bf16[1,512]{1,0:T(2,128)(2,1)}, u32[]{:S(2)}) copy-start(bf16[1,512]{1,0:T(2,128)(2,1)} %param.24) | copy-start | bytes 3076
  25.8 8.8 %copy-start.12 = (bf16[3,3,1,256]{3,1,2,0:T(4,128)(2,1)S(1)}, bf16[3,3,1,256]{3,1,2,0:T(4,128)(2,1)}, u32[]{:S(2)}) copy-start(bf16[3,3,1,256]{3,1,2,0:T(4,128)(2,1)} %param.33) | copy-start | bytes 13828
  25.8 9.6 %copy-start.37 = (bf16[1,256]{1,0:T(2,128)(2,1)S(1)}, bf16[1,256]{1,0:T(2,128)(2,1)}, u32[]{:S(2)}) copy-start(bf16[1,256]{1,0:T(2,128)(2,1)} %param.25) | copy-start | bytes 1540
  25.8 20.2 %copy-start.22 = (bf16[4,1,256]{2,0,1:T(4,128)(2,1)S(1)}, bf16[4,1,256]{2,0,1:T(4,128)(2,1)}, u32[]{:S(2)}) copy-start(bf16[4,1,256]{2,0,1:T(4,128)(2,1)} %param.23) | copy-start | bytes 6148
  25.8 20.8 %copy-start.19 = (bf16[4,1,512]{2,0,1:T(4,128)(2,1)S(1)}, bf16[4,1,512]{2,0,1:T(4,128)(2,1)}, u32[]{:S(2)}) copy-start(bf16[4,1,512]{2,0,1:T(4,128)(2,1)} %param.22) | copy-start | bytes 12292
  36.1 101.9 %copy-start.23 = (f32[1,8]{1,0:T(1,128)S(1)}, f32[1,8]{1,0:T(1,128)}, u32[]{:S(2)}) copy-start(f32[1,8]{1,0:T(1,128)} %param.26) | copy-start | bytes 100
  36.1 101.9 %copy-start.25 = (f32[1,8]{1,0:T(1,128)S(1)}, f32[1,8]{1,0:T(1,128)}, u32[]{:S(2)}) copy-start(f32[1,8]{1,0:T(1,128)} %param.27) | copy-start | bytes 100
  130.0 24.4 %copy-start.2 = (bf16[512,1288]{0,1:T(8,128)(2,1)}, bf16[512,1288]{0,1:T(8,128)(2,1)S(1)}, u32[]{:S(2)}) copy-start(bf16[512,1288]{0,1:T(8,128)(2,1)S(1)} %convert_bitcast_fusion) | copy-start | bytes 3956740
  130.0 14.9 %copy-start.30 = (f32[1,512]{1,0:T(1,128)S(1)}, f32[1,512]{1,0:T(1,128)}, u32[]{:S(2)}) copy-start(f32[1,512]{1,0:T(1,128)} %add.428) | copy-start | bytes 6148
  130.2 14.8 %copy-start.31 = (s32[512]{0:T(512)S(1)}, s32[512]{0:T(512)}, u32[]{:S(2)}) copy-start(s32[512]{0:T(512)} %get-tuple-element.29) | copy-start | bytes 6148
  130.2 14.8 %copy-start.32 = (f32[1,1,512]{2,0,1:T(1,128)S(1)}, f32[1,1,512]{2,0,1:T(1,128)}, u32[]{:S(2)}) copy-start(f32[1,1,512]{2,0,1:T(1,128)} %get-tuple-element.41) | copy-start | bytes 6148
  130.2 14.8 %copy-start.33 = (f32[1,1,512]{2,0,1:T(1,128)S(1)}, f32[1,1,512]{2,0,1:T(1,128)}, u32[]{:S(2)}) copy-start(f32[1,1,512]{2,0,1:T(1,128)} %get-tuple-element.42) | copy-start | bytes 6148
  130.2 14.8 %copy-start.34 = (f32[1,1,512]{2,0,1:T(1,128)S(1)}, f32[1,1,512]{2,0,1:T(1,128)}, u32[]{:S(2)}) copy-start(f32[1,1,512]{2,0,1:T(1,128)} %get-tuple-element.43) | copy-start | bytes 6148
  130.2 14.8 %copy-start.35 = (f32[1,1,512]{2,0,1:T(1,128)S(1)}, f32[1,1,512]{2,0,1:T(1,128)}, u32[]{:S(2)}) copy-start(f32[1,1,512]{2,0,1:T(1,128)} %get-tuple-element.44) | copy-start | bytes 6148
  130.2 14.8 %copy-start.41 = (pred[512]{0:T(512)(128)(4,1)S(1)}, pred[512]{0:T(512)(128)(4,1)}, u32[]{:S(2)}) copy-start(pred[512]{0:T(512)(128)(4,1)} %get-tuple-element.51) | copy-start | bytes 1540
  130.2 14.8 %copy-start.42 = (pred[512]{0:T(512)(128)(4,1)S(1)}, pred[512]{0:T(512)(128)(4,1)}, u32[]{:S(2)}) copy-start(pred[512]{0:T(512)(128)(4,1)} %get-tuple-element.52) | copy-start | bytes 1540
  130.2 14.8 %copy-start.43 = (pred[512]{0:T(512)(128)(4,1)S(1)}, pred[512]{0:T(512)(128)(4,1)}, u32[]{:S(2)}) copy-start(pred[512]{0:T(512)(128)(4,1)} %get-tuple-element.53) | copy-start | bytes 1540
  130.2 14.7 %collective-permute-start = (bf16[3,512]{0,1:T(8,128)(2,1)S(1)}, bf16[3,512]{0,1:T(8,128)(2,1)}, u32[]{:S(2)}, u32[]{:S(2)}) collective-permute-start(bf16[3,512]{0,1:T(8,128)(2,1)S(1)} %slice_select_fusion), channel_id=1, source_target_pairs={{0,8},{8,16},{16,24},{24,32},{32,40},{40,48},{48,56},{56,64},{64,7... | collective-permute-start | bytes 9224 | tf_op jit(solution)/shard_map/ppermute | solution.py:15
  135.5 7.7 %collective-permute-start.1 = (bf16[3,256]{0,1:T(8,128)(2,1)}, bf16[3,256]{0,1:T(8,128)(2,1)S(1)}, u32[]{:S(2)}, u32[]{:S(2)}) collective-permute-start(bf16[3,256]{0,1:T(8,128)(2,1)} %slice_select_fusion.1), channel_id=1, source_target_pairs={{0,8},{8,16},{16,24},{24,32},{32,40},{40,48},{48,56},{56,64},{64,7... | collective-permute-start | bytes 4616 | tf_op jit(solution)/shard_map/ppermute | solution.py:15
  140.0 0.8 copy-start.16
  147.7 22.4 %copy-start.4 = (bf16[512,512]{0,1:T(8,128)(2,1)}, bf16[512,512]{0,1:T(8,128)(2,1)S(1)}, u32[]{:S(2)}) copy-start(bf16[512,512]{0,1:T(8,128)(2,1)S(1)} %multiply_convert_fusion.1) | copy-start | bytes 1572868
  147.7 6.8 %copy-start.24 = (f32[1,8]{1,0:T(1,128)S(1)}, f32[1,8]{1,0:T(1,128)}, u32[]{:S(2)}) copy-start(f32[1,8]{1,0:T(1,128)} %param.26) | copy-start | bytes 100
  147.7 6.8 %copy-start.26 = (f32[1,8]{1,0:T(1,128)S(1)}, f32[1,8]{1,0:T(1,128)}, u32[]{:S(2)}) copy-start(f32[1,8]{1,0:T(1,128)} %param.27) | copy-start | bytes 100
  147.7 21.2 %copy-start.28 = (pred[3]{0:T(512)(128)(4,1)S(1)}, pred[3]{0:T(512)(128)(4,1)}, u32[]{:S(2)}) copy-start(pred[3]{0:T(512)(128)(4,1)} %broadcast_compare_fusion.5) | copy-start | bytes 13
  147.7 21.3 %copy-start.20 = (s32[1024]{0:T(1024)S(1)}, s32[1024]{0:T(1024)}, u32[]{:S(2)}) copy-start(s32[1024]{0:T(1024)} %pad_clamp_fusion.2) | copy-start | bytes 12292
  147.8 22.4 %copy-start.27 = (pred[512]{0:T(512)(128)(4,1)S(1)}, pred[512]{0:T(512)(128)(4,1)}, u32[]{:S(2)}) copy-start(pred[512]{0:T(512)(128)(4,1)} %broadcast_compare_fusion.1) | copy-start | bytes 1540
  151.5 10.7 %collective-permute-start.7 = (f32[8,65,128]{2,1,0:T(8,128)}, f32[8,65,128]{2,1,0:T(8,128)}, u32[]{:S(2)}, u32[]{:S(2)}) collective-permute-start(f32[8,65,128]{2,1,0:T(8,128)} %pad_maximum_fusion.8), channel_id=1, source_target_pairs={{8,0},{16,8},{24,16},{32,24},{40,32},{48,40},{56,48},{64,56},{72,6... | collective-permute-start | bytes 798728 | tf_op jit(solution)/shard_map/ppermute | solution.py:15
  166.2 48.6 %copy-start.40 = (pred[4]{0:T(512)(128)(4,1)S(1)}, pred[4]{0:T(512)(128)(4,1)}, u32[]{:S(2)}) copy-start(pred[4]{0:T(512)(128)(4,1)} %iota_compare_fusion.16) | copy-start | bytes 16
  167.0 17.9 %collective-permute-start.8 = (f32[8,65,128]{2,1,0:T(8,128)}, f32[8,65,128]{2,1,0:T(8,128)S(1)}, u32[]{:S(2)}, u32[]{:S(2)}) collective-permute-start(f32[8,65,128]{2,1,0:T(8,128)} %pad_maximum_fusion.9), channel_id=1, source_target_pairs={{16,0},{24,8},{32,16},{40,24},{48,32},{56,40},{64,48},{72,56},{80,... | collective-permute-start | bytes 798728 | tf_op jit(solution)/shard_map/ppermute | solution.py:15
  170.2 56.9 %copy-start.17 = (f32[8,4]{0,1:T(4,128)S(1)}, f32[8,4]{0,1:T(4,128)}, u32[]{:S(2)}) copy-start(f32[8,4]{0,1:T(4,128)} %copy-done.16) | copy-start | bytes 388
  184.9 6.6 %copy-start.6 = (f32[8,65,128]{2,1,0:T(8,128)}, f32[8,65,128]{2,1,0:T(8,128)S(1)}, u32[]{:S(2)}) copy-start(f32[8,65,128]{2,1,0:T(8,128)S(1)} %collective-permute-done.8) | copy-start | bytes 798724
  187.3 20.9 %collective-permute-start.9 = (f32[8,65,128]{2,1,0:T(8,128)}, f32[8,65,128]{2,1,0:T(8,128)}, u32[]{:S(2)}, u32[]{:S(2)}) collective-permute-start(f32[8,65,128]{2,1,0:T(8,128)} %pad_maximum_fusion.10), channel_id=1, source_target_pairs={{32,0},{40,8},{48,16},{56,24},{64,32},{72,40},{80,48},{88,56},{96,... | collective-permute-start | bytes 798728 | tf_op jit(solution)/shard_map/ppermute | solution.py:15
  192.9 38.7 %copy-start.7 = (f32[8,65,128]{2,1,0:T(8,128)S(1)}, f32[8,65,128]{2,1,0:T(8,128)}, u32[]{:S(2)}) copy-start(f32[8,65,128]{2,1,0:T(8,128)} %copy-done.6) | copy-start | bytes 798724
  192.9 43.0 %copy-start.3 = (f32[3,1,8,64,128]{4,3,2,1,0:T(8,128)S(1)}, f32[3,1,8,64,128]{4,3,2,1,0:T(8,128)}, u32[]{:S(2)}) copy-start(f32[3,1,8,64,128]{4,3,2,1,0:T(8,128)} %param.31) | copy-start | bytes 2359300
  212.9 9.7 %collective-permute-start.10 = (f32[8,65,128]{2,1,0:T(8,128)}, f32[8,65,128]{2,1,0:T(8,128)S(1)}, u32[]{:S(2)}, u32[]{:S(2)}) collective-permute-start(f32[8,65,128]{2,1,0:T(8,128)} %pad_maximum_fusion.11), channel_id=1, source_target_pairs={{64,0},{72,8},{80,16},{88,24},{96,32},{104,40},{112,48},{120,56},{... | collective-permute-start | bytes 798728 | tf_op jit(solution)/shard_map/ppermute | solution.py:15
  216.7 11.2 %collective-permute-start.2 = (f32[8,65,128]{2,1,0:T(8,128)}, f32[8,65,128]{2,1,0:T(8,128)S(1)}, u32[]{:S(2)}, u32[]{:S(2)}) collective-permute-start(f32[8,65,128]{2,1,0:T(8,128)} %pad_maximum_fusion.3), channel_id=1, source_target_pairs={{0,8},{8,16},{16,24},{24,32},{32,40},{40,48},{48,56},{56,64},{64,7... | collective-permute-start | bytes 798728 | tf_op jit(solution)/shard_map/ppermute | solution.py:15
  225.1 6.5 %collective-permute-start.11 = (f32[8,65,128]{2,1,0:T(8,128)}, f32[8,65,128]{2,1,0:T(8,128)}, u32[]{:S(2)}, u32[]{:S(2)}) collective-permute-start(f32[8,65,128]{2,1,0:T(8,128)} %pad_maximum_fusion.12), channel_id=1, source_target_pairs={{128,0},{136,8},{144,16},{152,24},{160,32},{168,40},{176,48},{184,... | collective-permute-start | bytes 798728 | tf_op jit(solution)/shard_map/ppermute | solution.py:15
  227.9 24.5 %copy-start.8 = (f32[8,65,128]{2,1,0:T(8,128)}, f32[8,65,128]{2,1,0:T(8,128)S(1)}, u32[]{:S(2)}) copy-start(f32[8,65,128]{2,1,0:T(8,128)S(1)} %collective-permute-done.2) | copy-start | bytes 798724
  232.5 22.9 %copy-start.15 = (f32[512,3]{0,1:T(4,128)S(1)}, f32[512,3]{0,1:T(4,128)}, u32[]{:S(2)}) copy-start(f32[512,3]{0,1:T(4,128)} %copy.86) | copy-start | bytes 18436
  233.9 18.0 %collective-permute-start.3 = (f32[8,65,128]{2,1,0:T(8,128)S(1)}, f32[8,65,128]{2,1,0:T(8,128)S(1)}, u32[]{:S(2)}, u32[]{:S(2)}) collective-permute-start(f32[8,65,128]{2,1,0:T(8,128)S(1)} %pad_maximum_fusion.4), channel_id=1, source_target_pairs={{0,16},{8,24},{16,32},{24,40},{32,48},{40,56},{48,64},{56,72},{64,... | collective-permute-start | bytes 798728 | tf_op jit(solution)/shard_map/ppermute | solution.py:15
  237.2 41.8 %copy-start.5 = (bf16[512,512]{0,1:T(8,128)(2,1)S(1)}, bf16[512,512]{0,1:T(8,128)(2,1)}, u32[]{:S(2)}) copy-start(bf16[512,512]{0,1:T(8,128)(2,1)} %copy-done.4) | copy-start | bytes 1572868
  237.3 41.8 %copy-start.10 = (pred[512,512]{1,0:T(8,128)(4,1)S(1)}, pred[512,512]{1,0:T(8,128)(4,1)}, u32[]{:S(2)}) copy-start(pred[512,512]{1,0:T(8,128)(4,1)} %fusion.46) | copy-start | bytes 786436
  237.3 41.8 %copy-start.18 = (f32[8,512]{1,0:T(8,128)S(1)}, f32[8,512]{1,0:T(8,128)}, u32[]{:S(2)}) copy-start(f32[8,512]{1,0:T(8,128)} %get-tuple-element.34) | copy-start | bytes 49156
  252.4 18.8 %collective-permute-start.4 = (f32[8,65,128]{2,1,0:T(8,128)S(1)}, f32[8,65,128]{2,1,0:T(8,128)S(1)}, u32[]{:S(2)}, u32[]{:S(2)}) collective-permute-start(f32[8,65,128]{2,1,0:T(8,128)S(1)} %pad_maximum_fusion.5), channel_id=1, source_target_pairs={{0,32},{8,40},{16,48},{24,56},{32,64},{40,72},{48,80},{56,88},{64,... | collective-permute-start | bytes 798728 | tf_op jit(solution)/shard_map/ppermute | solution.py:15
  271.5 14.7 %collective-permute-start.5 = (f32[8,65,128]{2,1,0:T(8,128)S(1)}, f32[8,65,128]{2,1,0:T(8,128)S(1)}, u32[]{:S(2)}, u32[]{:S(2)}) collective-permute-start(f32[8,65,128]{2,1,0:T(8,128)S(1)} %pad_maximum_fusion.6), channel_id=1, source_target_pairs={{0,64},{8,72},{16,80},{24,88},{32,96},{40,104},{48,112},{56,120},{... | collective-permute-start | bytes 798728 | tf_op jit(solution)/shard_map/ppermute | solution.py:15
  279.1 8.8 %copy-start.38 = (pred[3]{0:T(512)(128)(4,1)S(1)}, pred[3]{0:T(512)(128)(4,1)}, u32[]{:S(2)}) copy-start(pred[3]{0:T(512)(128)(4,1)} %get-tuple-element.58) | copy-start | bytes 13
  279.1 8.8 %copy-start.39 = (pred[3]{0:T(512)(128)(4,1)S(1)}, pred[3]{0:T(512)(128)(4,1)}, u32[]{:S(2)}) copy-start(pred[3]{0:T(512)(128)(4,1)} %get-tuple-element.59) | copy-start | bytes 13
  279.1 17.7 %copy-start.9 = (f32[8,65,128]{2,1,0:T(8,128)S(1)}, f32[8,65,128]{2,1,0:T(8,128)}, u32[]{:S(2)}) copy-start(f32[8,65,128]{2,1,0:T(8,128)} %copy-done.8) | copy-start | bytes 798724
  279.1 17.7 %copy-start.13 = (f32[512,8]{0,1:T(8,128)S(1)}, f32[512,8]{0,1:T(8,128)}, u32[]{:S(2)}) copy-start(f32[512,8]{0,1:T(8,128)} %get-tuple-element.23) | copy-start | bytes 49156
  279.1 17.7 %copy-start.44 = (f32[1,8]{1,0:T(1,128)S(1)}, f32[1,8]{1,0:T(1,128)}, u32[]{:S(2)}) copy-start(f32[1,8]{1,0:T(1,128)} %param.28) | copy-start | bytes 100
  286.6 17.2 %copy-start.36 = (f32[1,512]{1,0:T(1,128)S(1)}, f32[1,512]{1,0:T(1,128)}, u32[]{:S(2)}) copy-start(f32[1,512]{1,0:T(1,128)} %param.29) | copy-start | bytes 6148
  286.6 10.2 %collective-permute-start.6 = (f32[8,65,128]{2,1,0:T(8,128)S(1)}, f32[8,65,128]{2,1,0:T(8,128)S(1)}, u32[]{:S(2)}, u32[]{:S(2)}) collective-permute-start(f32[8,65,128]{2,1,0:T(8,128)S(1)} %pad_maximum_fusion.7), channel_id=1, source_target_pairs={{0,128},{8,136},{16,144},{24,152},{32,160},{40,168},{48,176},{56,1... | collective-permute-start | bytes 798728 | tf_op jit(solution)/shard_map/ppermute | solution.py:15
  296.8 11.2 %copy-start.1 = (bf16[1024,4,256]{2,1,0:T(4,128)(2,1)S(1)}, bf16[1024,4,256]{2,1,0:T(4,128)(2,1)}, u32[]{:S(2)}) copy-start(bf16[1024,4,256]{2,1,0:T(4,128)(2,1)} %param.20) | copy-start | bytes 6291460
Sparse Core Ops, SparseCore 0:
  26.0 102.1 reduce-scatter.1
